TPU v7x, 256 devices: a whole 4x4x8 slice. The times are simulated.
256 devices in a mesh: dp: 64 (over x, y_hi, z), tensor: 4 (over y_lo, core).
Axes of the slice: x: 4, y: 4 (y_hi: 2, y_lo: 2; y = y_hi * 2 + y_lo), z: 8, core: 2. Of those that a mesh axis runs over, the one named last changes fastest.
Arguments:
- residual: bfloat16 [512, 64, 4096], P('dp', None, 'tensor'), may hold values from -128 to 128
- queries: bfloat16 [512, 64, 4096], P('dp', None, 'tensor'), may hold values from -30 to 30
- attn_keys: bfloat16 [512, 64, 512], P('dp', None, 'tensor'), may hold values from -6 to 6
- values: bfloat16 [512, 64, 512], P('dp', None, 'tensor'), may hold values from -6 to 6
- out_weight: bfloat16 [4096, 4096], P('tensor'), may hold values from -0.09375 to 0.09375
- norm_gain: float32 [4096], P('tensor'), may hold values from 0.1 to 1.9
- probe_weight: float32 [4096, 64], P('tensor'), may hold values from -0.09375 to 0.09375
- partner_slot: int32 [512], P('dp'), may hold values from 0 to 7, as said below
- patch_list: int32 [512, 64, 2], P('dp', 'tensor'), may hold values from 0 to 63, as said below
- concept_labels: int32 [512, 64], P('dp'), may hold values from 0 to 63
Outputs:
- attn_out: bfloat16 [512, 64, 4096], P('dp', None, 'tensor')
- logits: float32 [512, 64, 64], P('dp')
- probe_grad: float32 [4096, 64], P('tensor')
Inputs may be any that keep to these rules, and one draw needn't show every extreme that they name: Prompt j of device i of dp, for i below 32, is paired with prompt partner_slot of it on device i + 32, and that prompt's partner_slot is j; on each device the values are a permutation. `patch_list`: each entry is (head, position). A prompt's list equals its partner's, entry for entry. Its entries are distinct, and entries k * 16 to (k + 1) * 16 - 1 name heads of the k-th block of 8 consecutive heads.
All inputs are finite; a program needn't handle non-finite values.
Results may differ from a plain program's by a relative error of at most 0.01.
Values may be sent and summed in bfloat16 or wider, within the bound.
No kernel may reach another device: no remote copies, remote signals or barrier semaphores. Data moves between devices by JAX's collectives and lax.ppermute only.
A program may use at most 128 MiB of HBM per device.

v0:
```python
import math
import jax
import jax.numpy as jnp
from jax import lax
from jax.sharding import PartitionSpec as P

DW = 4096
HDIM = 128
norm_epsilon = 1e-05


def passed_along(block, axis, distance):
    devices = range(lax.axis_size(axis))
    route = [((i - distance) % len(devices), i) for i in devices]
    return lax.ppermute(block, axis, route)


def attend(queries, attn_keys, values):
    prompt_count = queries.shape[0]
    seq_length = queries.shape[1]
    local_kv = attn_keys.shape[2] // HDIM
    local_heads = queries.shape[2] // HDIM
    group_size = local_heads // local_kv
    query_blocks = queries.reshape(prompt_count, seq_length, local_kv, group_size, HDIM)
    key_blocks = attn_keys.reshape(prompt_count, seq_length, local_kv, HDIM)
    value_blocks = values.reshape(prompt_count, seq_length, local_kv, HDIM)
    scores = jnp.einsum(
        "pqkgd,pskd->pkgqs", query_blocks, key_blocks, preferred_element_type=jnp.float32
    ) / math.sqrt(HDIM)
    causal = jnp.arange(seq_length)[:, None] >= jnp.arange(seq_length)[None, :]
    scores = jnp.where(causal, scores, -jnp.inf)
    highest = jnp.max(scores, axis=-1, keepdims=True)
    exponent = jnp.exp(scores - highest)
    weights = (exponent / jnp.sum(exponent, axis=-1, keepdims=True)).astype(jnp.bfloat16)
    mixed_rows = jnp.einsum(
        "pkgqs,pskd->pqkgd", weights, value_blocks, preferred_element_type=jnp.float32
    )
    return mixed_rows.astype(jnp.bfloat16).reshape(prompt_count, seq_length, local_heads, HDIM)


def per_device(
    residual,
    queries,
    attn_keys,
    values,
    out_weight,
    norm_gain,
    probe_weight,
    partner_slot,
    patch_list,
    concept_labels,
):
    prompt_count = residual.shape[0]
    seq_length = residual.shape[1]
    feature_count = residual.shape[2]
    token_count = prompt_count * seq_length
    heads_out = attend(queries, attn_keys, values)
    local_heads = heads_out.shape[2]
    head_ids = patch_list[..., 0] % local_heads
    pos_ids = patch_list[..., 1]
    row_ids = jnp.broadcast_to(jnp.arange(prompt_count, dtype=jnp.int32)[:, None], head_ids.shape)
    patch_mask = (
        jnp.zeros((prompt_count, seq_length, local_heads), dtype=bool)
        .at[row_ids, pos_ids, head_ids]
        .set(True)
    )
    half_way = lax.axis_size("dp") // 2
    arrived = passed_along(heads_out, "dp", half_way)
    entry_values = arrived[partner_slot][row_ids, pos_ids, head_ids]
    incoming = jnp.zeros_like(heads_out).at[row_ids, pos_ids, head_ids].set(entry_values)
    patched = jnp.where(patch_mask[..., None], incoming, heads_out)
    partial_value = jnp.dot(
        patched.reshape(token_count, -1), out_weight, preferred_element_type=jnp.float32
    )
    attn_local = lax.psum_scatter(
        partial_value.astype(jnp.bfloat16), "tensor", scatter_dimension=1, tiled=True
    )
    hidden = residual.reshape(token_count, feature_count).astype(jnp.float32) + attn_local.astype(
        jnp.float32
    )
    square_local = jnp.sum(hidden * hidden, axis=1)
    scaled = hidden * norm_gain
    square_sum = lax.psum(square_local, "tensor")
    inverse_rms = lax.rsqrt(square_sum / DW + norm_epsilon)
    normed = scaled * inverse_rms[:, None]
    logit_part = jnp.dot(
        normed, probe_weight, precision=lax.Precision.HIGHEST, preferred_element_type=jnp.float32
    )
    logits = lax.psum(logit_part.astype(jnp.bfloat16), "tensor").astype(jnp.float32)
    classes = jnp.arange(probe_weight.shape[1], dtype=jnp.int32)
    target = (concept_labels.reshape(token_count)[:, None] == classes[None, :]).astype(jnp.float32)
    error = jax.nn.sigmoid(logits) - target
    total_tokens = token_count * lax.axis_size("dp")
    grad_local = lax.dot_general(
        normed,
        error,
        (((0,), (0,)), ((), ())),
        precision=lax.Precision.HIGHEST,
        preferred_element_type=jnp.float32,
    ) / math.sqrt(total_tokens)
    probe_grad = lax.psum(grad_local, "dp")
    return (
        attn_local.reshape(prompt_count, seq_length, feature_count),
        logits.reshape(prompt_count, seq_length, -1),
        probe_grad,
    )


def solution(mesh):
    return jax.shard_map(
        per_device,
        mesh=mesh,
        in_specs=(
            P("dp", None, "tensor"),
            P("dp", None, "tensor"),
            P("dp", None, "tensor"),
            P("dp", None, "tensor"),
            P("tensor", None),
            P("tensor"),
            P("tensor", None),
            P("dp"),
            P("dp", "tensor", None),
            P("dp", None),
        ),
        out_specs=(P("dp", None, "tensor"), P("dp", None, None), P("tensor", None)),
        check_vma=False,
    )
```

profile of v0, /device:TPU:8, one launch (start us, length us, event | category | flops | bytes accessed | tf_op | source)
XLA Modules:
  0.0 822.0 jit_solution(9259078480574834374)
XLA Ops:
  7.2 0.0 copy-start
  7.2 0.0 reduce-scatter.2.cloned.1.call-start
  7.2 1.2 copy-done
  8.4 2.1 fusion.33
  10.5 0.5 fusion
  11.0 0.0 copy-done.8
  11.0 0.0 copy-start.5
  11.0 0.6 fusion.3
  11.7 0.0 copy-start.1
  11.7 0.0 copy-start.10
  11.7 3.1 collective-permute-start
  14.8 0.0 copy-done.5
  14.8 0.5 broadcast.168
  15.3 0.7 fusion.32
  16.0 0.1 reshape.81
  16.1 0.1 reshape.87
  16.2 8.5 %scatter_fusion = pred[8,64,8]{1,2,0:T(8,128)(4,1)S(1)} fusion(pred[8,64,8]{1,2,0:T(8,128)(4,1)S(1)} %broadcast_in_dim.23, s32[128]{0:T(128)S(1)} %reshape.87, pred[128]{0:T(512)(128)(4,1)S(1)} %broadcast.130), kind=kCustom, calls=%fused_computation.2 | custom fusion | bytes 1920 | tf_op jit(solution)/shard_map/scatter | solution.py:65
  24.7 0.0 copy-done.10
  24.8 13.4 %collective-permute-done = bf16[8,64,8,128]{3,1,2,0:T(8,128)(2,1)S(1)} collective-permute-done((bf16[8,64,8,128]{3,1,2,0:T(8,128)(2,1)S(1)}, bf16[8,64,8,128]{3,1,2,0:T(8,128)(2,1)S(1)}, u32[]{:S(2)}, u32[]{:S(2)}) %collective-permute-start) | collective-permute-done | bytes 1048608 | tf_op jit(solution)/shard_map/ppermute | solution.py:15
  38.2 0.7 gather_fusion
  38.9 0.7 copy.19
  39.6 1.2 gather_fusion.1
  40.9 0.1 broadcast_in_dim.27
  41.0 8.0 scatter_fusion.1
  49.0 1.8 copy_select_fusion
  50.8 0.7 copy.21
  51.5 9.4 %convolution_convert_fusion = bf16[512,4096]{1,0:T(8,128)(2,1)} fusion(bf16[1024,4096]{1,0:T(8,128)(2,1)} %param.14, bf16[64,8,8,128]{3,2,1,0:T(8,128)(2,1)S(1)} %bitcast.52), kind=kOutput, calls=%fused_computation.4 | convolution fusion | flops 4297064448 | bytes 13631488 | tf_op jit(solution)/shard_map/dot_general | solution.py:72
  60.9 0.0 reduce-scatter.2.cloned.1.call-update
  60.9 0.0 copy-start.7
  60.9 0.0 copy-start.9
  60.9 0.0 copy-start.6
  61.0 0.0 all-reduce.3.cloned.1.call-start
  61.0 49.1 %reduce-scatter.2.cloned.1.call-done = bf16[512,1024]{1,0:T(8,128)(2,1)} async-done(((bf16[512,4096]{1,0:T(8,128)(2,1)}), bf16[512,1024]{1,0:T(8,128)(2,1)}) %reduce-scatter.2.cloned.1.call-update) | async-done | bytes 1048592 | tf_op jit(solution)/shard_map/reduce_scatter | solution.py:75
  110.2 1.7 multiply_reduce_fusion
  111.9 7.7 psum.21
  119.6 0.0 copy-done.9
  119.6 0.0 copy-done.3
  119.7 3.1 fusion.5
  122.8 0.0 all-reduce.3.cloned.1.call-update
  122.8 0.0 all-reduce.5.cloned.1.call-start
  122.9 0.1 eq.17
  122.9 40.9 %all-reduce.3.cloned.1.call-done = bf16[512,64]{0,1:T(8,128)(2,1)} async-done(((bf16[512,64]{0,1:T(8,128)(2,1)}), bf16[512,64]{0,1:T(8,128)(2,1)}) %all-reduce.3.cloned.1.call-update) | async-done | bytes 65552 | tf_op jit(solution)/shard_map/psum | solution.py:89
  163.9 3.5 fusion.4
  167.3 0.0 all-reduce.5.cloned.1.call-update
  167.4 0.0 copy-done.4
  167.4 0.8 copy.26
  168.2 645.6 %all-reduce.5.cloned.1.call-done = f32[1024,64]{0,1:T(8,128)} async-done(((f32[1024,64]{0,1:T(8,128)}), f32[1024,64]{0,1:T(8,128)}) %all-reduce.5.cloned.1.call-update) | async-done | bytes 262160 | tf_op jit(solution)/shard_map/psum | solution.py:101
  813.8 1.7 copy.44
  (15 shorter events, 0.1 us)
Async XLA Ops:
  7.2 1.2 copy-start
  7.2 103.0 %reduce-scatter.2.cloned.1.call-start = ((), (), s32[]{:S(2)}) async-start(), calls=%async_computation.1 | async-start | bytes 5242880 | tf_op jit(solution)/shard_map/reduce_scatter | solution.py:75
  8.4 2.6 copy-start.8
  11.0 3.8 copy-start.5
  11.7 13.1 %copy-start.1 = (bf16[8,64,8,128]{3,1,2,0:T(8,128)(2,1)}, bf16[8,64,8,128]{3,1,2,0:T(8,128)(2,1)S(1)}, u32[]{:S(2)}) copy-start(bf16[8,64,8,128]{3,1,2,0:T(8,128)(2,1)S(1)} %fusion.3) | copy-start | bytes 3145732
  11.7 13.0 %copy-start.10 = (s32[8]{0:T(128)S(1)}, s32[8]{0:T(128)}, u32[]{:S(2)}) copy-start(s32[8]{0:T(128)} %param.17) | copy-start | bytes 100
  11.7 26.5 %collective-permute-start = (bf16[8,64,8,128]{3,1,2,0:T(8,128)(2,1)S(1)}, bf16[8,64,8,128]{3,1,2,0:T(8,128)(2,1)S(1)}, u32[]{:S(2)}, u32[]{:S(2)}) collective-permute-start(bf16[8,64,8,128]{3,1,2,0:T(8,128)(2,1)S(1)} %fusion.3), channel_id=1, source_target_pairs={{128,0},{132,4},{136,8},{140,12},{144,16},{148,20},{152,24},{156,2... | collective-permute-start | bytes 3145736 | tf_op jit(solution)/shard_map/ppermute | solution.py:15
  60.9 49.3 %copy-start.2 = (bf16[8,64,1024]{2,1,0:T(8,128)(2,1)S(1)}, bf16[8,64,1024]{2,1,0:T(8,128)(2,1)}, u32[]{:S(2)}) copy-start(bf16[8,64,1024]{2,1,0:T(8,128)(2,1)} %param.10) | copy-start | bytes 3145732
  60.9 58.7 %copy-start.7 = (f32[1024,64]{0,1:T(8,128)S(1)}, f32[1024,64]{0,1:T(8,128)}, u32[]{:S(2)}) copy-start(f32[1024,64]{0,1:T(8,128)} %param.16) | copy-start | bytes 786436
  60.9 58.7 %copy-start.9 = (f32[1024]{0:T(1024)S(1)}, f32[1024]{0:T(1024)}, u32[]{:S(2)}) copy-start(f32[1024]{0:T(1024)} %param.15) | copy-start | bytes 12292
  60.9 61.9 %copy-start.6 = (s32[8,64]{1,0:T(8,128)S(1)}, s32[8,64]{1,0:T(8,128)}, u32[]{:S(2)}) copy-start(s32[8,64]{1,0:T(8,128)} %param.19) | copy-start | bytes 6148
  61.0 102.9 %all-reduce.3.cloned.1.call-start = ((), (), s32[]{:S(2)}) async-start(), calls=%async_computation.2 | async-start | bytes 131072 | tf_op jit(solution)/shard_map/psum | solution.py:89
  110.2 9.5 %copy-start.3 = (bf16[512,1024]{1,0:T(8,128)(2,1)S(1)}, bf16[512,1024]{1,0:T(8,128)(2,1)}, u32[]{:S(2)}) copy-start(bf16[512,1024]{1,0:T(8,128)(2,1)} %reduce-scatter.2.cloned.1.call-done) | copy-start | bytes 3145732
  122.8 691.0 %all-reduce.5.cloned.1.call-start = ((), (), s32[]{:S(2)}) async-start(), calls=%async_computation.3 | async-start | bytes 524288 | tf_op jit(solution)/shard_map/psum | solution.py:101
  163.9 3.5 copy-start.4
Sparse Core Ops, SparseCore 0:
  61.0 49.0 reduce-scatter.1
  122.9 40.9 all-reduce.2
  167.5 646.2 all-reduce.4
where the time goes:
time: 822 us
  waiting for transfers between devices  749 us (91%)
  local copies, waits for them, and re-layouts  24.4 us (3%)
  matrix products  18.7 us (2%)
  between operations  14 us (2%)
    psum x1, waiting for transfers between devices, per_device(): probe_grad = lax.psum(grad_local, 'dp')  646 us
    reduce_scatter x1, waiting for transfers between devices, per_device(): lax.psum_scatter(partial_value.astype(jnp.bfloat16), 'tensor', scatter_di...  49.1 us
    psum x1, waiting for transfers between devices, per_device(): lax.psum(logit_part.astype(jnp.bfloat16), 'tensor').astype(jnp.float32)  40.9 us
  transfers between devices with their start and end apart: 4, of which 4 were waited for; matrix products, arithmetic and copies ran while one was open for 1% of the time, Pallas kernels for 0%

commit v1 on v0

--- a/solution.py
+++ b/solution.py
@@ -86,7 +86,9 @@
     logit_part = jnp.dot(
         normed, probe_weight, precision=lax.Precision.HIGHEST, preferred_element_type=jnp.float32
     )
-    logits = lax.psum(logit_part.astype(jnp.bfloat16), "tensor").astype(jnp.float32)
+    logits = jnp.sum(lax.all_gather(logit_part.astype(jnp.bfloat16), "tensor"), axis=0).astype(
+        jnp.float32
+    )
     classes = jnp.arange(probe_weight.shape[1], dtype=jnp.int32)
     target = (concept_labels.reshape(token_count)[:, None] == classes[None, :]).astype(jnp.float32)
     error = jax.nn.sigmoid(logits) - target

time: 822 us -> 787 us (0.957)
  waiting for transfers between devices: 749 us -> 707 us
    psum x1 -> x0, waiting for transfers between devices: 40.9 us -> none  [per_device(): lax.psum(logit_part.astype(jnp.bfloat16), 'tensor').astype(jnp.float32)]
  transfers between devices with their start and end apart: 4 -> 3, of which waited for: 4 -> 3; matrix products, arithmetic and copies ran while one was open for 1% -> 1% of each run, Pallas kernels for 0% -> 0%
where the time goes in v1:
time: 787 us
  waiting for transfers between devices  707 us (90%)
  local copies, waits for them, and re-layouts  26.2 us (3%)
  matrix products  17.1 us (2%)
  between operations  14.2 us (2%)
  blocking collectives  14 us (2%)
    psum x1, waiting for transfers between devices, per_device(): probe_grad = lax.psum(grad_local, 'dp')  645 us
    reduce_scatter x1, waiting for transfers between devices, per_device(): lax.psum_scatter(partial_value.astype(jnp.bfloat16), 'tensor', scatter_di...  48.5 us
  transfers between devices with their start and end apart: 3, of which 3 were waited for; matrix products, arithmetic and copies ran while one was open for 1% of the time, Pallas kernels for 0%

profile of v1, /device:TPU:8, one launch (start us, length us, event | category | flops | bytes accessed | tf_op | source)
XLA Modules:
  0.0 786.6 jit_solution(3456478017747611399)
XLA Ops:
  7.2 0.0 copy-start
  7.2 0.0 reduce-scatter.2.cloned.1.call-start
  7.2 1.2 copy-done
  8.4 2.1 fusion.33
  10.5 0.5 fusion
  11.0 0.0 copy-done.7
  11.0 0.0 copy-start.4
  11.0 0.6 fusion.3
  11.7 0.0 copy-start.1
  11.7 0.0 copy-start.9
  11.7 3.1 collective-permute-start
  14.8 0.0 copy-done.4
  14.8 0.5 broadcast.168
  15.4 0.7 fusion.32
  16.0 0.1 reshape.82
  16.1 0.1 reshape.88
  16.2 8.5 %scatter_fusion = pred[8,64,8]{1,2,0:T(8,128)(4,1)S(1)} fusion(pred[8,64,8]{1,2,0:T(8,128)(4,1)S(1)} %broadcast_in_dim.23, s32[128]{0:T(128)S(1)} %reshape.88, pred[128]{0:T(512)(128)(4,1)S(1)} %broadcast.130), kind=kCustom, calls=%fused_computation.2 | custom fusion | bytes 1920 | tf_op jit(solution)/shard_map/scatter | solution.py:65
  24.7 0.0 copy-done.9
  24.7 0.0 copy-done.1
  24.8 13.4 %collective-permute-done = bf16[8,64,8,128]{3,1,2,0:T(8,128)(2,1)S(1)} collective-permute-done((bf16[8,64,8,128]{3,1,2,0:T(8,128)(2,1)S(1)}, bf16[8,64,8,128]{3,1,2,0:T(8,128)(2,1)S(1)}, u32[]{:S(2)}, u32[]{:S(2)}) %collective-permute-start) | collective-permute-done | bytes 1048608 | tf_op jit(solution)/shard_map/ppermute | solution.py:15
  38.2 0.7 gather_fusion
  38.9 0.7 copy.23
  39.6 1.2 gather_fusion.1
  40.9 0.1 broadcast_in_dim.27
  41.0 8.0 %scatter_fusion.1 = bf16[8,64,8,128]{3,2,1,0:T(8,128)(2,1)S(1)} fusion(bf16[8,64,8,128]{3,2,1,0:T(8,128)(2,1)S(1)} %broadcast_in_dim.27, s32[128]{0:T(128)S(1)} %reshape.88, bf16[128,128]{1,0:T(8,128)(2,1)S(1)} %gather_fusion.1), kind=kCustom, calls=%fused_computation.3 | custom fusion | bytes 99840 | tf_op jit(solution)/shard_map/scatter | solution.py:70
  49.0 1.8 copy_select_fusion
  50.8 0.7 copy.25
  51.5 9.4 %convolution_convert_fusion = bf16[512,4096]{1,0:T(8,128)(2,1)} fusion(bf16[1024,4096]{1,0:T(8,128)(2,1)} %param.14, bf16[64,8,8,128]{3,2,1,0:T(8,128)(2,1)S(1)} %bitcast.54), kind=kOutput, calls=%fused_computation.4 | convolution fusion | flops 4297064448 | bytes 13631488 | tf_op jit(solution)/shard_map/dot_general | solution.py:72
  60.9 0.0 reduce-scatter.2.cloned.1.call-update
  60.9 0.0 copy-start.6
  60.9 0.0 copy-start.8
  60.9 0.0 all-reduce.2.cloned.1.call-start
  61.0 0.6 copy-done.5
  61.6 0.1 eq.17
  61.7 48.5 %reduce-scatter.2.cloned.1.call-done = bf16[512,1024]{1,0:T(8,128)(2,1)} async-done(((bf16[512,4096]{1,0:T(8,128)(2,1)}), bf16[512,1024]{1,0:T(8,128)(2,1)}) %reduce-scatter.2.cloned.1.call-update) | async-done | bytes 1048592 | tf_op jit(solution)/shard_map/reduce_scatter | solution.py:75
  110.2 0.0 copy-done.2
  110.2 1.7 multiply_reduce_fusion
  111.9 7.7 psum.14
  119.6 0.0 copy-done.6
  119.7 2.5 fusion.5
  122.1 6.2 all-gather
  128.4 1.1 reshape.100
  129.5 0.3 reduce_sum.32
  129.8 2.6 fusion.4
  132.4 0.0 all-reduce.2.cloned.1.call-update
  132.4 0.8 copy.30
  133.2 644.9 %all-reduce.2.cloned.1.call-done = f32[1024,64]{0,1:T(8,128)} async-done(((f32[1024,64]{0,1:T(8,128)}), f32[1024,64]{0,1:T(8,128)}) %all-reduce.2.cloned.1.call-update) | async-done | bytes 262160 | tf_op jit(solution)/shard_map/psum | solution.py:103
  778.1 1.7 copy.47
  (13 shorter events, 0.1 us)
Async XLA Ops:
  7.2 1.2 copy-start
  7.2 103.0 %reduce-scatter.2.cloned.1.call-start = ((), (), s32[]{:S(2)}) async-start(), calls=%async_computation.1 | async-start | bytes 5242880 | tf_op jit(solution)/shard_map/reduce_scatter | solution.py:75
  8.4 2.6 copy-start.7
  11.0 3.8 copy-start.4
  11.7 13.1 %copy-start.1 = (bf16[8,64,8,128]{3,1,2,0:T(8,128)(2,1)}, bf16[8,64,8,128]{3,1,2,0:T(8,128)(2,1)S(1)}, u32[]{:S(2)}) copy-start(bf16[8,64,8,128]{3,1,2,0:T(8,128)(2,1)S(1)} %fusion.3) | copy-start | bytes 3145732
  11.7 13.0 %copy-start.9 = (s32[8]{0:T(128)S(1)}, s32[8]{0:T(128)}, u32[]{:S(2)}) copy-start(s32[8]{0:T(128)} %param.17) | copy-start | bytes 100
  11.7 26.5 %collective-permute-start = (bf16[8,64,8,128]{3,1,2,0:T(8,128)(2,1)S(1)}, bf16[8,64,8,128]{3,1,2,0:T(8,128)(2,1)S(1)}, u32[]{:S(2)}, u32[]{:S(2)}) collective-permute-start(bf16[8,64,8,128]{3,1,2,0:T(8,128)(2,1)S(1)} %fusion.3), channel_id=1, source_target_pairs={{128,0},{132,4},{136,8},{140,12},{144,16},{148,20},{152,24},{156,2... | collective-permute-start | bytes 3145736 | tf_op jit(solution)/shard_map/ppermute | solution.py:15
  60.9 0.7 copy-start.5
  60.9 49.3 %copy-start.2 = (bf16[8,64,1024]{2,1,0:T(8,128)(2,1)S(1)}, bf16[8,64,1024]{2,1,0:T(8,128)(2,1)}, u32[]{:S(2)}) copy-start(bf16[8,64,1024]{2,1,0:T(8,128)(2,1)} %param.10) | copy-start | bytes 3145732
  60.9 58.7 %copy-start.6 = (f32[1024,64]{0,1:T(8,128)S(1)}, f32[1024,64]{0,1:T(8,128)}, u32[]{:S(2)}) copy-start(f32[1024,64]{0,1:T(8,128)} %param.16) | copy-start | bytes 786436
  60.9 58.7 %copy-start.8 = (f32[1024]{0:T(1024)S(1)}, f32[1024]{0:T(1024)}, u32[]{:S(2)}) copy-start(f32[1024]{0:T(1024)} %param.15) | copy-start | bytes 12292
  60.9 717.2 %all-reduce.2.cloned.1.call-start = ((), (), s32[]{:S(2)}) async-start(), calls=%async_computation.2 | async-start | bytes 524288 | tf_op jit(solution)/shard_map/psum | solution.py:103
  110.2 9.5 %copy-start.3 = (bf16[512,1024]{1,0:T(8,128)(2,1)S(1)}, bf16[512,1024]{1,0:T(8,128)(2,1)}, u32[]{:S(2)}) copy-start(bf16[512,1024]{1,0:T(8,128)(2,1)} %reduce-scatter.2.cloned.1.call-done) | copy-start | bytes 3145732
Sparse Core Ops, SparseCore 0:
  61.0 49.0 reduce-scatter.1
  132.5 645.5 all-reduce.1
